TPU v7x, 32 devices: a whole 2x2x4 slice. The times are simulated.
32 devices in a mesh: groups: 2 (over y), seq: 4 (over z), tensor: 4 (over x, core).
Axes of the slice: x: 2, y: 2, z: 4, core: 2. Of those that a mesh axis runs over, the one named last changes fastest.
Arguments:
- x_in: bfloat16 [4096, 5120], P(('groups', 'seq'), 'tensor'), parts along dimension 0, may hold values from -6 to 6
- z_gate: bfloat16 [4096, 5120], P(('groups', 'seq'), 'tensor'), parts along dimension 0, may hold values from -32 to 32
- bc_in: bfloat16 [4096, 256], P(('groups', 'seq')), parts along dimension 0, may hold values from -6 to 6
- step_size: float32 [80, 4096], P('tensor', ('groups', 'seq')), parts along dimension 1, may hold values from 0 to 0.4
- log_keep: float32 [80, 4096], P('tensor', ('groups', 'seq')), parts along dimension 1, may hold values from -1 to 0
- skip_gain: float32 [80], P('tensor'), may hold values from 0.5 to 2
- conv_x: bfloat16 [4, 5120], P(None, 'tensor'), may hold values from -3 to 3
- conv_bc: bfloat16 [4, 256], replicated, may hold values from -3 to 3
- norm_gain: float32 [5120], P('tensor'), may hold values from 0.1 to 1.9
- seg_ends: int32 [1024], P(('groups', 'seq')), parts along dimension 0, may hold values from 0 to 2047, as said below
- pool_query: bfloat16 [320, 5120], P(('groups', 'seq'), 'tensor'), parts along dimension 0, may hold values from -64 to 64
- pool_start: int32 [320], P(('groups', 'seq')), parts along dimension 0, may hold values from 0 to 255, as said below
- pool_stop: int32 [320], P(('groups', 'seq')), parts along dimension 0, may hold values from 64 to 512
Outputs:
- mixed_seq: bfloat16 [4096, 5120], P(('groups', 'seq'), 'tensor'), parts along dimension 0
- pooled: float32 [320, 5120], P(('groups', 'seq'), 'tensor'), parts along dimension 0
There are 2 independent parts, one for each index of `groups`. A program takes and returns all parts, laid end to end along the dimension named above; an argument that names none is the same for every part. Nothing has to cross between parts.
Inputs may be any that keep to these rules, and one draw needn't show every extreme that they name: The tokens fall into blocks of 512; block b holds exactly the 128 segment ends seg_ends[b * 128] to seg_ends[(b + 1) * 128 - 1], strictly increasing. pool_start < pool_stop for every pooled row.
All inputs are finite; a program needn't handle non-finite values.
Results may differ from a plain program's by a relative error of at most 0.039.
Values may be sent and summed in bfloat16 or wider, within the bound.
No kernel may reach another device: no remote copies, remote signals or barrier semaphores. Data moves between devices by JAX's collectives and lax.ppermute only.
A program may use at most 64 MiB of HBM per device.

v0:
```python
import math
import jax
import jax.numpy as jnp
from jax import lax
from jax.sharding import PartitionSpec as P

STRETCH = 256
POOL_HEADS = 32
EPSILON = 1e-05
MASKED = -1e30


def passed_along(value, axis, steps):
    count = lax.axis_size(axis)
    leading, last = (max(0, -steps), min(count, count - steps))
    return lax.ppermute(value, axis, [(source, source + steps) for source in range(leading, last)])


def silu_act(values):
    return values / (1.0 + jnp.exp(-values))


def causal_conv(before, current, weights):
    kernel_width = weights.shape[0]
    length = current.shape[0]
    padded = jnp.concatenate([before, current], axis=0)
    summed = jnp.zeros(current.shape, jnp.float32)
    for offset in range(kernel_width):
        summed = summed + padded[offset : offset + length].astype(jnp.float32) * weights[
            offset
        ].astype(jnp.float32)
    return silu_act(summed).astype(jnp.bfloat16)


def stretch_local(x_block, b_block, c_block, step_block, keep_block):
    block_len = x_block.shape[0]
    cumul_keep = jnp.cumsum(keep_block, axis=1)
    lower_mask = lax.broadcasted_iota(jnp.int32, (block_len, block_len), 0) >= lax.broadcasted_iota(
        jnp.int32, (block_len, block_len), 1
    )
    inner_prod = jnp.einsum("is,js->ij", c_block, b_block, preferred_element_type=jnp.float32)
    spread = cumul_keep[:, :, None] - cumul_keep[:, None, :]
    decay_mask = jnp.where(lower_mask[None], jnp.exp(jnp.where(lower_mask[None], spread, 0.0)), 0.0)
    mixing = (decay_mask * inner_prod[None] * step_block[:, None, :]).astype(jnp.bfloat16)
    intra_part = jnp.einsum("hij,jhp->ihp", mixing, x_block, preferred_element_type=jnp.float32)
    tail_weight = jnp.exp(cumul_keep[:, -1:] - cumul_keep) * step_block
    weighted = (tail_weight.T[:, :, None] * x_block.astype(jnp.float32)).astype(jnp.bfloat16)
    stretch_state = jnp.einsum("jhp,js->hps", weighted, b_block, preferred_element_type=jnp.float32)
    return (intra_part, stretch_state, cumul_keep)


def combine(earlier, later):
    return (earlier[0] * jnp.exp(later[1])[:, None, None] + later[0], earlier[1] + later[1])


def exclusive_scan(state, decay, axis):
    count = lax.axis_size(axis)
    window = (state, decay)
    before = (jnp.zeros_like(state), jnp.zeros_like(decay))
    shift = 1
    while shift < count:
        sent_state = passed_along(window[0].astype(jnp.bfloat16), axis, shift)
        sent_decay = passed_along(window[1], axis, shift)
        received = (sent_state.astype(jnp.float32), sent_decay)
        before = combine(received, before)
        if shift * 2 < count:
            window = combine(received, window)
        shift *= 2
    return before[0]


def read_state(c_block, state_in):
    state_high = state_in.astype(jnp.bfloat16)
    state_low = (state_in - state_high.astype(jnp.float32)).astype(jnp.bfloat16)
    high_part = jnp.einsum("is,hps->ihp", c_block, state_high, preferred_element_type=jnp.float32)
    low_part = jnp.einsum("is,hps->ihp", c_block, state_low, preferred_element_type=jnp.float32)
    return high_part + low_part


def local(
    x_in,
    z_gate,
    bc_in,
    step_size,
    log_keep,
    skip_gain,
    conv_x,
    conv_bc,
    norm_gain,
    seg_ends,
    pool_query,
    pool_start,
    pool_stop,
):
    tok_rows = x_in.shape[0]
    channels = x_in.shape[1]
    heads_local = step_size.shape[0]
    head_width = channels // heads_local
    state_width = bc_in.shape[1] // 2
    rim_rows = conv_x.shape[0] - 1
    seq_count = lax.axis_size("seq")
    queries_all = lax.all_gather(pool_query, "seq", axis=0, tiled=True)
    start_all = lax.all_gather(pool_start, "seq", axis=0, tiled=True)
    stop_all = lax.all_gather(pool_stop, "seq", axis=0, tiled=True)
    edge_rows = jnp.concatenate([x_in[tok_rows - rim_rows :], bc_in[tok_rows - rim_rows :]], axis=1)
    before = passed_along(edge_rows, "seq", 1)
    x_conv = causal_conv(before[:, :channels], x_in, conv_x)
    bc_conv = causal_conv(before[:, channels:], bc_in, conv_bc)
    b_mat = bc_conv[:, :state_width]
    c_mat = bc_conv[:, state_width:]
    x_heads = x_conv.reshape(tok_rows, heads_local, head_width)
    stretch_count = tok_rows // STRETCH
    entry_state = jnp.zeros((heads_local, head_width, state_width), jnp.float32)
    decay_total = jnp.zeros((heads_local,), jnp.float32)
    saved_parts = []
    for block_index in range(stretch_count):
        first_row = block_index * STRETCH
        last_row = first_row + STRETCH
        intra_part, stretch_state, cumul_keep = stretch_local(
            x_heads[first_row:last_row],
            b_mat[first_row:last_row],
            c_mat[first_row:last_row],
            step_size[:, first_row:last_row],
            log_keep[:, first_row:last_row],
        )
        saved_parts.append((intra_part, cumul_keep, entry_state, decay_total))
        entry_state = jnp.exp(cumul_keep[:, -1])[:, None, None] * entry_state + stretch_state
        decay_total = decay_total + cumul_keep[:, -1]
    incoming = exclusive_scan(entry_state, decay_total, "seq")
    pieces_out = []
    for block_index in range(stretch_count):
        intra_part, cumul_keep, entry_part, decay_part = saved_parts[block_index]
        first_row = block_index * STRETCH
        state_in = entry_part + jnp.exp(decay_part)[:, None, None] * incoming
        from_state = read_state(c_mat[first_row : first_row + STRETCH], state_in)
        pieces_out.append(intra_part + jnp.exp(cumul_keep).T[:, :, None] * from_state)
    ssd_out = jnp.concatenate(pieces_out, axis=0) + skip_gain[None, :, None] * x_heads.astype(
        jnp.float32
    )
    gated = ssd_out.reshape(tok_rows, channels) * silu_act(z_gate.astype(jnp.float32))
    square_sum = lax.psum(jnp.sum(gated * gated, axis=1), "tensor")
    width_all = channels * lax.axis_size("tensor")
    mixed_seq = (
        gated * lax.rsqrt(square_sum / width_all + EPSILON)[:, None] * norm_gain[None, :]
    ).astype(jnp.bfloat16)
    local_ends = seg_ends - lax.axis_index("seq") * tok_rows
    summaries = jnp.take(mixed_seq, local_ends, axis=0)
    pool_heads_local = POOL_HEADS // lax.axis_size("tensor")
    pool_width = channels // pool_heads_local
    scale_factor = 1.0 / math.sqrt(pool_width)
    pools_local = pool_query.shape[0]
    pools_all = queries_all.shape[0]
    segs_local = summaries.shape[0]
    queries = queries_all.reshape(pools_all, pool_heads_local, pool_width)
    seg_index = lax.axis_index("seq") * segs_local + lax.iota(jnp.int32, segs_local)
    inside = (seg_index[None, :] >= start_all[:, None]) & (seg_index[None, :] < stop_all[:, None])
    keys_block = summaries.reshape(segs_local, pool_heads_local, pool_width)
    logits = (
        jnp.einsum("pad,rad->apr", queries, keys_block, preferred_element_type=jnp.float32)
        * scale_factor
    )
    logits = jnp.where(inside[None], logits, MASKED)
    peak = jnp.max(logits, axis=2)
    expo = jnp.where(inside[None], jnp.exp(logits - peak[:, :, None]), 0.0)
    denom = jnp.sum(expo, axis=2)
    numer = jnp.einsum(
        "apr,rad->pad", expo.astype(jnp.bfloat16), keys_block, preferred_element_type=jnp.float32
    )
    numer_sent = lax.all_to_all(
        numer.reshape(pools_all, channels).astype(jnp.bfloat16), "seq", 0, 0, tiled=True
    )
    stats = jnp.concatenate([peak.T, denom.T], axis=1)
    stats_sent = lax.all_to_all(stats, "seq", 0, 0, tiled=True)
    numer_parts = numer_sent.astype(jnp.float32).reshape(
        seq_count, pools_local, pool_heads_local, pool_width
    )
    stats_parts = stats_sent.reshape(seq_count, pools_local, 2, pool_heads_local)
    peak_parts = stats_parts[:, :, 0]
    denom_parts = stats_parts[:, :, 1]
    peak_all = jnp.max(peak_parts, axis=0)
    rescale = jnp.exp(peak_parts - peak_all[None])
    denom_all = jnp.sum(rescale * denom_parts, axis=0)
    numer_all = jnp.sum(rescale[:, :, :, None] * numer_parts, axis=0)
    pooled = (numer_all / denom_all[:, :, None]).reshape(pools_local, channels)
    return (mixed_seq, pooled)


def solution(mesh):
    in_specs = (
        P(("groups", "seq"), "tensor"),
        P(("groups", "seq"), "tensor"),
        P(("groups", "seq"), None),
        P("tensor", ("groups", "seq")),
        P("tensor", ("groups", "seq")),
        P("tensor"),
        P(None, "tensor"),
        P(),
        P("tensor"),
        P(("groups", "seq")),
        P(("groups", "seq"), "tensor"),
        P(("groups", "seq")),
        P(("groups", "seq")),
    )
    out_specs = (P(("groups", "seq"), "tensor"), P(("groups", "seq"), "tensor"))
    return jax.shard_map(local, mesh=mesh, in_specs=in_specs, out_specs=out_specs, check_vma=False)
```

profile of v0, /device:TPU:0, one launch (start us, length us, event | category | flops | bytes accessed | tf_op | source)
XLA Modules:
  0.0 130.5 jit_solution(8809013497023641823)
XLA Ops:
  0.6 0.8 slice.127
  1.4 0.7 slice.126
  2.2 5.0 %collective-permute-start = (bf16[3,1536]{1,0:T(4,128)(2,1)S(1)}, bf16[3,1536]{1,0:T(4,128)(2,1)S(1)}, u32[]{:S(2)}, u32[]{:S(2)}) collective-permute-start(bf16[3,1536]{1,0:T(4,128)(2,1)S(1)} %pad_maximum_fusion.3), channel_id=1, source_target_pairs={{0,4},{4,8},{8,12},{1,5},{5,9},{9,13},{2,6},{6,10},{10,14},{3,7},{... | collective-permute-start | bytes 27656 | tf_op jit(solution)/shard_map/ppermute | solution.py:16
  7.2 0.8 fusion.82
  7.9 0.6 reduce-window.14
  10.6 3.5 %collective-permute-start.3 = (f32[20]{0:T(128)S(1)}, f32[20]{0:T(128)S(1)}, u32[]{:S(2)}, u32[]{:S(2)}) collective-permute-start(f32[20]{0:T(128)S(1)} %get-tuple-element.33), channel_id=1, source_target_pairs={{0,4},{4,8},{8,12},{1,5},{5,9},{9,13},{2,6},{6,10},{10,14},{3,7},{... | collective-permute-start | bytes 248 | tf_op jit(solution)/shard_map/ppermute | solution.py:16
  14.1 0.7 iota_compare_fusion
  14.8 0.9 convert_reduce_fusion.3
  15.7 1.5 %fusion.81 = (f32[20,256]{1,0:T(8,128)}, f32[256,20]{0,1:T(8,128)}, f32[256,20]{0,1:T(8,128)}, f32[20,256]{1,0:T(8,128)}, f32[256,20]{0,1:T(8,128)}, /*index=5*/f32[256,20]{0,1:T(8,128)}) fusion(f32[20,512]{1,0:T(8,128)} %param.16, f32[20,256]{1,0:T(8,128)S(1)} %bitcast.92, f32[20]{0:T(128)S(1)} %get-tuple-element.39, f32[20,256]{1,0:T(8,128)S(1)} %bitcast.95, ...), kind=kLoop, calls=%fused_computation.140 | loop fusion | flops 20480 | bytes 204960 | tf_op jit(solution)/shard_map/slice | solution.py:123
  17.2 1.4 %slice_convert_fusion.3 = (f32[1,256]{1,0:T(1,128)}, f32[1,256]{1,0:T(1,128)}, f32[1,256]{1,0:T(1,128)}, f32[1,256]{1,0:T(1,128)}) fusion(bf16[4,256]{1,0:T(4,128)(2,1)} %param.20), kind=kLoop, calls=%fused_computation.130 | loop fusion | flops 1024 | bytes 6144 | tf_op jit(solution)/shard_map/mul | solution.py:29
  18.6 15.2 %all_gather.11 = bf16[160,1280]{1,0:T(8,128)(2,1)S(1)} all-gather(bf16[40,1280]{1,0:T(8,128)(2,1)} %param.23), channel_id=1, replica_groups=mesh['groups'=2,'seq'=4,'tensor'=4] {'seq'}, dimensions={0}, use_global_device_ids=true | all-gather | bytes 512000 | tf_op jit(solution)/shard_map/all_gather | solution.py:102
  33.8 1.2 compare_and_fusion.1
  35.0 1.2 dynamic-slice
  36.8 0.9 dynamic-update-slice.1
  37.6 0.8 dynamic-update-slice
  38.5 6.6 %all-reduce.2 = (s32[160]{0:T(256)S(1)}, s32[160]{0:T(256)S(1)}) all-reduce(s32[160]{0:T(256)S(1)} %dynamic-update-slice.1, s32[160]{0:T(256)S(1)} %dynamic-update-slice), channel_id=1, replica_groups=mesh['groups'=2,'seq'=4,'tensor'=4] {'seq'}, use_global_device_ids=true, to_apply=%add.1 | all-reduce | flops 320 | bytes 2560
  45.0 0.7 compare_and_fusion
  45.7 0.7 mul.339
  46.5 1.7 %reshape.222 = bf16[160,8,160]{2,1,0:T(8,128)(2,1)} reshape(bf16[160,1280]{1,0:T(8,128)(2,1)S(1)} %all_gather.11) | data formatting | bytes 819200 | tf_op jit(solution)/shard_map/reshape | solution.py:154
  48.2 1.8 %divide_convert_fusion = bf16[512,1280]{1,0:T(8,128)(2,1)S(1)} fusion(bf16[512,1280]{1,0:T(8,128)(2,1)S(1)} %copy-done.1, bf16[3,1280]{1,0:T(4,128)(2,1)S(1)} %slice.166, f32[1280]{0:T(1024)S(1)} %get-tuple-element.4, f32[1280]{0:T(1024)S(1)} %get-tuple-element.5, f32[1280]{0:T(1024)S(1)} %get-tuple-element.3, f32[1280]{0:T(1024)S(1)} %get-tuple-element.2), kind=kLoop, calls=%fused_computation.23 | loop fusion | flops 15728640 | bytes 2649600 | tf_op jit(solution)/shard_map/convert_element_type | solution.py:32
  50.4 1.9 %divide_convert_fusion.1 = bf16[512,256]{1,0:T(8,128)(2,1)S(1)} fusion(bf16[512,256]{1,0:T(8,128)(2,1)} %param.15, bf16[3,256]{1,0:T(4,128)(2,1)S(1)} %slice.173, f32[256]{0:T(256)} %bitcast.104, f32[256]{0:T(256)} %bitcast.105, f32[256]{0:T(256)} %bitcast.103, f32[256]{0:T(256)} %bitcast.102), kind=kLoop, calls=%fused_computation.62 | loop fusion | flops 3145728 | bytes 529920 | tf_op jit(solution)/shard_map/convert_element_type | solution.py:32
  52.3 0.9 fusion.57
  53.5 1.1 convolution_add_fusion.3
  54.6 1.1 fusion.84
  55.7 3.3 %collective-permute-start.1 = (bf16[20,64,128]{2,1,0:T(8,128)(2,1)S(1)}, bf16[20,64,128]{2,1,0:T(8,128)(2,1)S(1)}, u32[]{:S(2)}, u32[]{:S(2)}) collective-permute-start(bf16[20,64,128]{2,1,0:T(8,128)(2,1)S(1)} %get-tuple-element.35), channel_id=1, source_target_pairs={{0,4},{4,8},{8,12},{1,5},{5,9},{9,13},{2,6},{6,10},{10,14},{3,7},{... | collective-permute-start | bytes 983048 | tf_op jit(solution)/shard_map/ppermute | solution.py:16
  59.1 1.7 %fusion.17 = f32[256,20,64]{0,2,1:T(8,128)S(1)} fusion(bf16[256,20,64]{0,2,1:T(8,128)(2,1)S(1)} %bitcast.88, f32[20,256]{1,0:T(8,128)S(1)} %copy-done.13, f32[256,256]{1,0:T(8,128)S(1)} %copy-done.4, f32[20,256]{1,0:T(8,128)S(1)} %bitcast.96, pred[256,256]{1,0:T(8,128)(4,1)S(1)} %copy-done.11), kind=kOutput, calls=%fused_computation.28 | convolution fusion | flops 175636480 | bytes 2334720 | tf_op jit(solution)/shard_map/hij,jhp->ihp/dot_general | solution.py:45
  60.9 3.9 %collective-permute-done.1 = bf16[20,64,128]{2,1,0:T(8,128)(2,1)S(1)} collective-permute-done((bf16[20,64,128]{2,1,0:T(8,128)(2,1)S(1)}, bf16[20,64,128]{2,1,0:T(8,128)(2,1)S(1)}, u32[]{:S(2)}, u32[]{:S(2)}) %collective-permute-start.1) | collective-permute-done | bytes 327712 | tf_op jit(solution)/shard_map/ppermute | solution.py:16
  65.0 10.0 %collective-permute-start.2 = (bf16[20,64,128]{2,1,0:T(8,128)(2,1)S(1)}, bf16[20,64,128]{2,1,0:T(8,128)(2,1)S(1)}, u32[]{:S(2)}, u32[]{:S(2)}) collective-permute-start(bf16[20,64,128]{2,1,0:T(8,128)(2,1)S(1)} %fusion.29), channel_id=1, source_target_pairs={{0,8},{4,12},{1,9},{5,13},{2,10},{6,14},{3,11},{7,15},{16,24},{20,... | collective-permute-start | bytes 983048 | tf_op jit(solution)/shard_map/ppermute | solution.py:16
  75.0 2.9 %fusion.18 = f32[256,20,64]{0,2,1:T(8,128)} fusion(bf16[256,20,64]{0,2,1:T(8,128)(2,1)S(1)} %bitcast.86, f32[20,256]{1,0:T(8,128)S(1)} %copy-done.12, f32[256,256]{1,0:T(8,128)S(1)} %fusion.61, f32[20,256]{1,0:T(8,128)S(1)} %bitcast.93, pred[256,256]{1,0:T(8,128)(4,1)S(1)} %copy-done.11), kind=kOutput, calls=%fused_computation.29 | convolution fusion | flops 175636480 | bytes 2334720 | tf_op jit(solution)/shard_map/hij,jhp->ihp/dot_general | solution.py:45
  77.9 1.6 %collective-permute-done.2 = bf16[20,64,128]{2,1,0:T(8,128)(2,1)S(1)} collective-permute-done((bf16[20,64,128]{2,1,0:T(8,128)(2,1)S(1)}, bf16[20,64,128]{2,1,0:T(8,128)(2,1)S(1)}, u32[]{:S(2)}, u32[]{:S(2)}) %collective-permute-start.2) | collective-permute-done | bytes 327712 | tf_op jit(solution)/shard_map/ppermute | solution.py:16
  79.9 1.5 %fusion.22 = f32[256,20,64]{0,2,1:T(8,128)} fusion(f32[256,20,64]{0,2,1:T(8,128)S(1)} %fusion.17, f32[256,20,64]{0,2,1:T(8,128)S(1)} %fusion.49, f32[256,20]{0,1:T(8,128)S(1)} %copy-done.10, bf16[512,256]{1,0:T(8,128)(2,1)S(1)} %divide_convert_fusion.1, f32[20,64,128]{2,1,0:T(8,128)S(1)} %convolution_add_fusion.3, ...), kind=kOutput, calls=%fused_computation.35 | convolution fusion | flops 86507520 | bytes 5334016 | tf_op jit(solution)/shard_map/is,hps->ihp/dot_general | solution.py:76
  81.4 1.7 %copy.69 = f32[256,1280]{1,0:T(8,128)S(1)} copy(f32[256,1280]{0,1:T(8,128)} %bitcast.84) | data formatting | bytes 2621440 | tf_op jit(solution)/shard_map/concatenate | solution.py:137
  83.5 0.9 copy-done.2
  84.4 2.2 %fusion.21 = f32[256,20,64]{0,2,1:T(8,128)} fusion(f32[256,20,64]{0,2,1:T(8,128)S(1)} %copy-done.2, f32[256,20,64]{0,2,1:T(8,128)S(1)} %fusion.38, f32[256,20]{0,1:T(8,128)} %get-tuple-element.25, bf16[20,64,128]{2,1,0:T(8,128)(2,1)S(1)} %collective-permute-done.1, bf16[20,64,128]{2,1,0:T(8,128)(2,1)S(1)} %collective-permute-done.2, f32[20]{0:T(128)S(1)} %exp.71, ...), kind=kOutput, calls=%fused_computation.34 | convolution fusion | flops 85688320 | bytes 4674048 | tf_op jit(solution)/shard_map/is,hps->ihp/dot_general | solution.py:75
  86.6 2.8 %copy.68 = f32[256,1280]{1,0:T(8,128)} copy(f32[256,1280]{0,1:T(8,128)} %bitcast.83) | data formatting | bytes 2621440 | tf_op jit(solution)/shard_map/concatenate | solution.py:137
  89.4 4.2 %multiply_reduce_fusion = (f32[512]{0:T(512)S(1)}, f32[512,1280]{1,0:T(8,128)}) fusion(bf16[512,1280]{1,0:T(8,128)(2,1)} %param.14, bf16[512,1280]{1,0:T(8,128)(2,1)S(1)} %divide_convert_fusion, f32[1280]{0:T(1024)S(1)} %mul.340, f32[256,1280]{1,0:T(8,128)S(1)} %copy.69, f32[256,1280]{1,0:T(8,128)} %copy.68), kind=kLoop, calls=%fused_computation.12 | loop fusion | flops 7208448 | bytes 7871488 | tf_op jit(solution)/shard_map/reduce_sum | solution.py:141
  93.7 5.8 %psum.7 = f32[512]{0:T(512)S(1)} all-reduce(f32[512]{0:T(512)S(1)} %get-tuple-element.12), channel_id=1, replica_groups=mesh['groups'=2,'seq'=4,'tensor'=4] {'tensor'}, use_global_device_ids=true, to_apply=%region_5.6 | all-reduce | flops 512 | bytes 4096 | tf_op jit(solution)/shard_map/psum | solution.py:141
  99.5 2.0 %multiply_convert_fusion.4 = bf16[512,1280]{1,0:T(8,128)(2,1)S(1)} fusion(f32[512,1280]{1,0:T(8,128)} %get-tuple-element.13, f32[1280]{0:T(1024)S(1)} %copy-done.14, f32[512]{0:T(512)S(1)} %add_rsqrt_fusion), kind=kLoop, calls=%fused_computation.11 | loop fusion | flops 1966080 | bytes 3939328 | tf_op jit(solution)/shard_map/convert_element_type | solution.py:145
  101.6 0.9 gather_fusion
  104.4 0.7 reshape.263
  105.1 4.7 %all-to-all-start = ((f32[4,1,640]{2,1,0:T(1,128)}), f32[4,1,640]{2,1,0:T(1,128)S(1)}, u32[]{:S(2)}, u32[]{:S(2)}) async-start(f32[4,1,640]{2,1,0:T(1,128)} %reshape.263), calls=%async_computation | async-start | bytes 20480 | tf_op jit(solution)/shard_map/all_to_all | solution.py:173
  110.7 1.4 %convert_element_type.154 = bf16[4,40,1280]{2,1,0:T(8,128)(2,1)} reshape(bf16[160,8,160]{2,1,0:T(8,128)(2,1)S(1)} %copy.75) | data formatting | bytes 819200 | tf_op jit(solution)/shard_map/convert_element_type | solution.py:170
  112.2 3.2 %all-to-all-done = f32[4,1,640]{2,1,0:T(1,128)S(1)} async-done(((f32[4,1,640]{2,1,0:T(1,128)}), f32[4,1,640]{2,1,0:T(1,128)S(1)}, u32[]{:S(2)}, u32[]{:S(2)}) %all-to-all-start) | async-done | bytes 10272 | tf_op jit(solution)/shard_map/all_to_all | solution.py:173
  115.3 3.5 %all-to-all-start.1 = ((bf16[4,40,1280]{2,1,0:T(8,128)(2,1)}), bf16[4,40,1280]{2,1,0:T(8,128)(2,1)S(1)}, u32[]{:S(2)}, u32[]{:S(2)}) async-start(bf16[4,40,1280]{2,1,0:T(8,128)(2,1)} %convert_element_type.154), calls=%async_computation.1 | async-start | bytes 819200 | tf_op jit(solution)/shard_map/all_to_all | solution.py:169
  119.3 0.7 reduce.18
  120.4 0.6 mul.355
  121.4 8.3 %all-to-all-done.1 = bf16[4,40,1280]{2,1,0:T(8,128)(2,1)S(1)} async-done(((bf16[4,40,1280]{2,1,0:T(8,128)(2,1)}), bf16[4,40,1280]{2,1,0:T(8,128)(2,1)S(1)}, u32[]{:S(2)}, u32[]{:S(2)}) %all-to-all-start.1) | async-done | bytes 409632 | tf_op jit(solution)/shard_map/all_to_all | solution.py:169
  129.7 0.7 div.33
  (94 shorter events, 8.1 us)
Async XLA Ops:
  0.6 47.6 %copy-start.1 = (bf16[512,1280]{1,0:T(8,128)(2,1)S(1)}, bf16[512,1280]{1,0:T(8,128)(2,1)}, u32[]{:S(2)}) copy-start(bf16[512,1280]{1,0:T(8,128)(2,1)} %param.13) | copy-start | bytes 3932164
  2.2 46.0 %collective-permute-start = (bf16[3,1536]{1,0:T(4,128)(2,1)S(1)}, bf16[3,1536]{1,0:T(4,128)(2,1)S(1)}, u32[]{:S(2)}, u32[]{:S(2)}) collective-permute-start(bf16[3,1536]{1,0:T(4,128)(2,1)S(1)} %pad_maximum_fusion.3), channel_id=1, source_target_pairs={{0,4},{4,8},{8,12},{1,5},{5,9},{9,13},{2,6},{6,10},{10,14},{3,7},{... | collective-permute-start | bytes 27656 | tf_op jit(solution)/shard_map/ppermute | solution.py:16
  8.9 9.7 %copy-start.6 = (f32[3,8,2,128]{3,1,2,0:T(8,128)}, f32[3,8,2,128]{3,1,2,0:T(8,128)S(1)}, u32[]{:S(2)}) copy-start(f32[3,8,2,128]{3,1,2,0:T(8,128)S(1)} %copy.80) | copy-start | bytes 73732
  9.8 8.8 %copy-start.8 = (f32[3,8,2,128]{3,1,2,0:T(8,128)}, f32[3,8,2,128]{3,1,2,0:T(8,128)S(1)}, u32[]{:S(2)}) copy-start(f32[3,8,2,128]{3,1,2,0:T(8,128)S(1)} %copy.81) | copy-start | bytes 73732
  10.6 37.6 %collective-permute-start.3 = (f32[20]{0:T(128)S(1)}, f32[20]{0:T(128)S(1)}, u32[]{:S(2)}, u32[]{:S(2)}) collective-permute-start(f32[20]{0:T(128)S(1)} %get-tuple-element.33), channel_id=1, source_target_pairs={{0,4},{4,8},{8,12},{1,5},{5,9},{9,13},{2,6},{6,10},{10,14},{3,7},{... | collective-permute-start | bytes 248 | tf_op jit(solution)/shard_map/ppermute | solution.py:16
  53.5 5.5 %copy-start.4 = (f32[256,256]{1,0:T(8,128)S(1)}, f32[256,256]{1,0:T(8,128)}, u32[]{:S(2)}) copy-start(f32[256,256]{1,0:T(8,128)} %fusion.57) | copy-start | bytes 786436
  53.5 5.5 %copy-start.9 = (f32[3,8,2,128]{3,1,2,0:T(8,128)S(1)}, f32[3,8,2,128]{3,1,2,0:T(8,128)}, u32[]{:S(2)}) copy-start(f32[3,8,2,128]{3,1,2,0:T(8,128)} %copy-done.8) | copy-start | bytes 73732
  53.5 5.5 %copy-start.11 = (pred[256,256]{1,0:T(8,128)(4,1)S(1)}, pred[256,256]{1,0:T(8,128)(4,1)}, u32[]{:S(2)}) copy-start(pred[256,256]{1,0:T(8,128)(4,1)} %iota_compare_fusion) | copy-start | bytes 196612
  53.5 5.5 %copy-start.13 = (f32[20,256]{1,0:T(8,128)S(1)}, f32[20,256]{1,0:T(8,128)}, u32[]{:S(2)}) copy-start(f32[20,256]{1,0:T(8,128)} %get-tuple-element.21) | copy-start | bytes 61444
  55.7 9.1 %collective-permute-start.1 = (bf16[20,64,128]{2,1,0:T(8,128)(2,1)S(1)}, bf16[20,64,128]{2,1,0:T(8,128)(2,1)S(1)}, u32[]{:S(2)}, u32[]{:S(2)}) collective-permute-start(bf16[20,64,128]{2,1,0:T(8,128)(2,1)S(1)} %get-tuple-element.35), channel_id=1, source_target_pairs={{0,4},{4,8},{8,12},{1,5},{5,9},{9,13},{2,6},{6,10},{10,14},{3,7},{... | collective-permute-start | bytes 983048 | tf_op jit(solution)/shard_map/ppermute | solution.py:16
  59.0 5.8 %copy-start.16 = (f32[20]{0:T(128)S(1)}, f32[20]{0:T(128)}, u32[]{:S(2)}) copy-start(f32[20]{0:T(128)} %get-tuple-element.32) | copy-start | bytes 244
  59.0 15.9 %copy-start.7 = (f32[3,8,2,128]{3,1,2,0:T(8,128)S(1)}, f32[3,8,2,128]{3,1,2,0:T(8,128)}, u32[]{:S(2)}) copy-start(f32[3,8,2,128]{3,1,2,0:T(8,128)} %copy-done.6) | copy-start | bytes 73732
  59.0 15.9 %copy-start.12 = (f32[20,256]{1,0:T(8,128)S(1)}, f32[20,256]{1,0:T(8,128)}, u32[]{:S(2)}) copy-start(f32[20,256]{1,0:T(8,128)} %get-tuple-element.18) | copy-start | bytes 61444
  65.0 14.5 %collective-permute-start.2 = (bf16[20,64,128]{2,1,0:T(8,128)(2,1)S(1)}, bf16[20,64,128]{2,1,0:T(8,128)(2,1)S(1)}, u32[]{:S(2)}, u32[]{:S(2)}) collective-permute-start(bf16[20,64,128]{2,1,0:T(8,128)(2,1)S(1)} %fusion.29), channel_id=1, source_target_pairs={{0,8},{4,12},{1,9},{5,13},{2,10},{6,14},{3,11},{7,15},{16,24},{20,... | collective-permute-start | bytes 983048 | tf_op jit(solution)/shard_map/ppermute | solution.py:16
  75.0 4.5 %copy-start.15 = (f32[20]{0:T(128)S(1)}, f32[20]{0:T(128)}, u32[]{:S(2)}) copy-start(f32[20]{0:T(128)} %get-tuple-element.30) | copy-start | bytes 244
  77.9 2.0 %copy-start.10 = (f32[256,20]{0,1:T(8,128)S(1)}, f32[256,20]{0,1:T(8,128)}, u32[]{:S(2)}) copy-start(f32[256,20]{0,1:T(8,128)} %get-tuple-element.24) | copy-start | bytes 61444
  83.1 1.3 %copy-start.2 = (f32[256,20,64]{0,2,1:T(8,128)S(1)}, f32[256,20,64]{0,2,1:T(8,128)}, u32[]{:S(2)}) copy-start(f32[256,20,64]{0,2,1:T(8,128)} %fusion.18) | copy-start | bytes 3932164
  89.4 10.1 %copy-start.14 = (f32[1280]{0:T(1024)S(1)}, f32[1280]{0:T(1024)}, u32[]{:S(2)}) copy-start(f32[1280]{0:T(1024)} %param.21) | copy-start | bytes 15364
  101.5 2.1 %copy-start = (bf16[512,1280]{1,0:T(8,128)(2,1)}, bf16[512,1280]{1,0:T(8,128)(2,1)S(1)}, u32[]{:S(2)}) copy-start(bf16[512,1280]{1,0:T(8,128)(2,1)S(1)} %multiply_convert_fusion.4) | copy-start | bytes 3932164
  101.5 1.6 %copy-start.3 = (bf16[160,8,160]{2,1,0:T(8,128)(2,1)S(1)}, bf16[160,8,160]{2,1,0:T(8,128)(2,1)}, u32[]{:S(2)}) copy-start(bf16[160,8,160]{2,1,0:T(8,128)(2,1)} %reshape.222) | copy-start | bytes 1228804
  101.6 1.6 %copy-start.5 = (pred[160,128]{1,0:T(8,128)(4,1)S(1)}, pred[160,128]{1,0:T(8,128)(4,1)}, u32[]{:S(2)}) copy-start(pred[160,128]{1,0:T(8,128)(4,1)} %compare_and_fusion) | copy-start | bytes 61444
  101.6 1.5 %copy-start.17 = (pred[128]{0:T(512)(128)(4,1)S(1)}, pred[128]{0:T(512)(128)(4,1)}, u32[]{:S(2)}) copy-start(pred[128]{0:T(512)(128)(4,1)} %get-tuple-element.10) | copy-start | bytes 388
  105.1 10.2 %all-to-all-start = ((f32[4,1,640]{2,1,0:T(1,128)}), f32[4,1,640]{2,1,0:T(1,128)S(1)}, u32[]{:S(2)}, u32[]{:S(2)}) async-start(f32[4,1,640]{2,1,0:T(1,128)} %reshape.263), calls=%async_computation | async-start | bytes 20480 | tf_op jit(solution)/shard_map/all_to_all | solution.py:173
  115.3 14.3 %all-to-all-start.1 = ((bf16[4,40,1280]{2,1,0:T(8,128)(2,1)}), bf16[4,40,1280]{2,1,0:T(8,128)(2,1)S(1)}, u32[]{:S(2)}, u32[]{:S(2)}) async-start(bf16[4,40,1280]{2,1,0:T(8,128)(2,1)} %convert_element_type.154), calls=%async_computation.1 | async-start | bytes 819200 | tf_op jit(solution)/shard_map/all_to_all | solution.py:169
where the time goes:
time: 132 us; the launch traced here: 130 us
  starting transfers between devices  29.8 us (23%)
  blocking collectives  27.6 us (21%)
  other arithmetic  20.7 us (16%)
  local copies, waits for them, and re-layouts  20.5 us (16%)
  waiting for transfers between devices  16.9 us (13%)
  matrix products  13.3 us (10%)
  between operations  1.74 us (1%)
    ppermute x4, starting transfers between devices, passed_along(): lax.ppermute(value, axis, [(source, source + steps) for source in range(l...  21.6 us
    all_gather x1, blocking collectives, local(): queries_all = lax.all_gather(pool_query, 'seq', axis=0, tiled=True)  15.2 us
    all_to_all x1, waiting for transfers between devices, local(): lax.all_to_all(numer.reshape(pools_all, channels).astype(jnp.bfloat16), '...  8.25 us
    unnamed x1, blocking collectives  6.55 us
    psum x1, blocking collectives, local(): square_sum = lax.psum(jnp.sum(gated * gated, axis=1), 'tensor')  5.81 us
    ppermute x4, waiting for transfers between devices, passed_along(): lax.ppermute(value, axis, [(source, source + steps) for source in range(l...  5.47 us
    unnamed x47, local copies, waits for them, and re-layouts  5.14 us
    all_to_all x1, starting transfers between devices, local(): stats_sent = lax.all_to_all(stats, 'seq', 0, 0, tiled=True)  4.65 us
  transfers between devices with their start and end apart: 6, of which 4 were waited for; matrix products, arithmetic and copies ran while one was open for 19% of the time, Pallas kernels for 0%

commit v1 on v0

--- a/solution.py
+++ b/solution.py
@@ -8,6 +8,22 @@
 POOL_HEADS = 32
 EPSILON = 1e-05
 MASKED = -1e30
+
+
+def swapped_with_each(x, axis, split, join):
+    ways, here = (lax.axis_size(axis), lax.axis_index(axis))
+    width = x.shape[split] // ways
+    shape = list(x.shape)
+    shape[split] = width
+    height = shape[join]
+    shape[join] = height * ways
+    full = jnp.zeros(shape, x.dtype)
+    for mask in range(ways):
+        part = lax.dynamic_slice_in_dim(x, (here ^ mask) * width, width, axis=split)
+        if mask:
+            part = lax.ppermute(part, axis, [(d, d ^ mask) for d in range(ways)])
+        full = lax.dynamic_update_slice_in_dim(full, part, (here ^ mask) * height, axis=join)
+    return full
 
 
 def passed_along(value, axis, steps):
@@ -166,8 +182,8 @@
     numer = jnp.einsum(
         "apr,rad->pad", expo.astype(jnp.bfloat16), keys_block, preferred_element_type=jnp.float32
     )
-    numer_sent = lax.all_to_all(
-        numer.reshape(pools_all, channels).astype(jnp.bfloat16), "seq", 0, 0, tiled=True
+    numer_sent = swapped_with_each(
+        numer.reshape(pools_all, channels).astype(jnp.bfloat16), "seq", 0, 0
     )
     stats = jnp.concatenate([peak.T, denom.T], axis=1)
     stats_sent = lax.all_to_all(stats, "seq", 0, 0, tiled=True)

time: 132 us -> 125 us (0.947)
  waiting for transfers between devices: 16.9 us -> 11 us
    all_to_all x1 -> x0, waiting for transfers between devices: 8.25 us -> none  [local(): lax.all_to_all(numer.reshape(pools_all, channels).astype(jnp.bfloat16), '...]
    ppermute x0 -> x3, starting transfers between devices: none -> 5.01 us  [swapped_with_each(): part = lax.ppermute(part, axis, [(d, d ^ mask) for d in range(ways)])]
    all_to_all x1 -> x0, starting transfers between devices: 3.46 us -> none  [local(): lax.all_to_all(numer.reshape(pools_all, channels).astype(jnp.bfloat16), '...]
    all_to_all x1, waiting for transfers between devices: 3.16 us -> 5.54 us  [local(): stats_sent = lax.all_to_all(stats, 'seq', 0, 0, tiled=True)]
    convert_element_type x2 -> x0, local copies, waits for them, and re-layouts: 1.99 us -> none  [local(): numer.reshape(pools_all, channels).astype(jnp.bfloat16)]
    unnamed x47 -> x51, local copies, waits for them, and re-layouts: 5.14 us -> 5.77 us
  transfers between devices with their start and end apart: 6 -> 8, of which waited for: 4 -> 3; matrix products, arithmetic and copies ran while one was open for 19% -> 18% of each run, Pallas kernels for 0% -> 0%
where the time goes in v1:
time: 125 us; the launch traced here: 124 us
  starting transfers between devices  30.3 us (24%)
  blocking collectives  27.6 us (22%)
  local copies, waits for them, and re-layouts  20.3 us (16%)
  other arithmetic  20.2 us (16%)
  matrix products  13.4 us (11%)
  waiting for transfers between devices  11 us (9%)
  between operations  1.77 us (1%)
    ppermute x4, starting transfers between devices, passed_along(): lax.ppermute(value, axis, [(source, source + steps) for source in range(l...  21.6 us
    all_gather x1, blocking collectives, local(): queries_all = lax.all_gather(pool_query, 'seq', axis=0, tiled=True)  15.2 us
    unnamed x1, blocking collectives  6.55 us
    psum x1, blocking collectives, local(): square_sum = lax.psum(jnp.sum(gated * gated, axis=1), 'tensor')  5.81 us
    unnamed x51, local copies, waits for them, and re-layouts  5.77 us
    all_to_all x1, waiting for transfers between devices, local(): stats_sent = lax.all_to_all(stats, 'seq', 0, 0, tiled=True)  5.54 us
    ppermute x4, waiting for transfers between devices, passed_along(): lax.ppermute(value, axis, [(source, source + steps) for source in range(l...  5.47 us
    ppermute x3, starting transfers between devices, swapped_with_each(): part = lax.ppermute(part, axis, [(d, d ^ mask) for d in range(ways)])  5.01 us
  transfers between devices with their start and end apart: 8, of which 3 were waited for; matrix products, arithmetic and copies ran while one was open for 18% of the time, Pallas kernels for 0%

profile of v1, /device:TPU:0, one launch (start us, length us, event | category | flops | bytes accessed | tf_op | source)
XLA Modules:
  0.0 124.5 jit_solution(18262248038066140282)
XLA Ops:
  0.6 0.8 slice.127
  1.4 0.7 slice.126
  2.2 5.0 %collective-permute-start = (bf16[3,1536]{1,0:T(4,128)(2,1)S(1)}, bf16[3,1536]{1,0:T(4,128)(2,1)S(1)}, u32[]{:S(2)}, u32[]{:S(2)}) collective-permute-start(bf16[3,1536]{1,0:T(4,128)(2,1)S(1)} %pad_maximum_fusion.3), channel_id=1, source_target_pairs={{0,4},{4,8},{8,12},{1,5},{5,9},{9,13},{2,6},{6,10},{10,14},{3,7},{... | collective-permute-start | bytes 27656 | tf_op jit(solution)/shard_map/ppermute | solution.py:32
  7.2 0.8 fusion.81
  7.9 0.6 reduce-window.14
  8.9 0.6 reduce-window.16
  10.6 3.5 %collective-permute-start.3 = (f32[20]{0:T(128)S(1)}, f32[20]{0:T(128)S(1)}, u32[]{:S(2)}, u32[]{:S(2)}) collective-permute-start(f32[20]{0:T(128)S(1)} %get-tuple-element.37), channel_id=1, source_target_pairs={{0,4},{4,8},{8,12},{1,5},{5,9},{9,13},{2,6},{6,10},{10,14},{3,7},{... | collective-permute-start | bytes 248 | tf_op jit(solution)/shard_map/ppermute | solution.py:32
  14.1 0.7 iota_compare_fusion
  14.8 0.9 convert_reduce_fusion.3
  15.7 1.5 %fusion.80 = (f32[20,256]{1,0:T(8,128)}, f32[256,20]{0,1:T(8,128)}, f32[256,20]{0,1:T(8,128)}, f32[20,256]{1,0:T(8,128)}, f32[256,20]{0,1:T(8,128)}, /*index=5*/f32[256,20]{0,1:T(8,128)}) fusion(f32[20,512]{1,0:T(8,128)} %param.16, f32[20,256]{1,0:T(8,128)S(1)} %bitcast.90, f32[20]{0:T(128)S(1)} %get-tuple-element.43, f32[20,256]{1,0:T(8,128)S(1)} %bitcast.93, ...), kind=kLoop, calls=%fused_computation.148 | loop fusion | flops 20480 | bytes 204960 | tf_op jit(solution)/shard_map/slice | solution.py:139
  17.2 1.4 %slice_convert_fusion.3 = (f32[1,256]{1,0:T(1,128)}, f32[1,256]{1,0:T(1,128)}, f32[1,256]{1,0:T(1,128)}, f32[1,256]{1,0:T(1,128)}) fusion(bf16[4,256]{1,0:T(4,128)(2,1)} %param.20), kind=kLoop, calls=%fused_computation.138 | loop fusion | flops 1024 | bytes 6144 | tf_op jit(solution)/shard_map/mul | solution.py:45
  18.6 15.2 %all_gather.11 = bf16[160,1280]{1,0:T(8,128)(2,1)S(1)} all-gather(bf16[40,1280]{1,0:T(8,128)(2,1)} %param.23), channel_id=1, replica_groups=mesh['groups'=2,'seq'=4,'tensor'=4] {'seq'}, dimensions={0}, use_global_device_ids=true | all-gather | bytes 512000 | tf_op jit(solution)/shard_map/all_gather | solution.py:118
  33.8 1.2 compare_and_fusion.1
  35.0 1.2 dynamic-slice
  36.8 0.9 dynamic-update-slice.1
  37.6 0.8 dynamic-update-slice
  38.5 6.6 %all-reduce.2 = (s32[160]{0:T(256)S(1)}, s32[160]{0:T(256)S(1)}) all-reduce(s32[160]{0:T(256)S(1)} %dynamic-update-slice.1, s32[160]{0:T(256)S(1)} %dynamic-update-slice), channel_id=1, replica_groups=mesh['groups'=2,'seq'=4,'tensor'=4] {'seq'}, use_global_device_ids=true, to_apply=%add.1 | all-reduce | flops 320 | bytes 2560
  45.0 0.7 compare_and_fusion
  45.7 0.7 mul.352
  46.5 1.7 %reshape.221 = bf16[160,8,160]{2,1,0:T(8,128)(2,1)} reshape(bf16[160,1280]{1,0:T(8,128)(2,1)S(1)} %all_gather.11) | data formatting | bytes 819200 | tf_op jit(solution)/shard_map/reshape | solution.py:170
  48.2 1.8 %divide_convert_fusion = bf16[512,1280]{1,0:T(8,128)(2,1)S(1)} fusion(bf16[512,1280]{1,0:T(8,128)(2,1)S(1)} %copy-done.1, bf16[3,1280]{1,0:T(4,128)(2,1)S(1)} %slice.166, f32[1280]{0:T(1024)S(1)} %get-tuple-element.4, f32[1280]{0:T(1024)S(1)} %get-tuple-element.5, f32[1280]{0:T(1024)S(1)} %get-tuple-element.3, f32[1280]{0:T(1024)S(1)} %get-tuple-element.2), kind=kLoop, calls=%fused_computation.23 | loop fusion | flops 15728640 | bytes 2649600 | tf_op jit(solution)/shard_map/convert_element_type | solution.py:48
  50.4 1.9 %divide_convert_fusion.1 = bf16[512,256]{1,0:T(8,128)(2,1)S(1)} fusion(bf16[512,256]{1,0:T(8,128)(2,1)} %param.15, bf16[3,256]{1,0:T(4,128)(2,1)S(1)} %slice.173, f32[256]{0:T(256)} %bitcast.102, f32[256]{0:T(256)} %bitcast.103, f32[256]{0:T(256)} %bitcast.101, f32[256]{0:T(256)} %bitcast.100), kind=kLoop, calls=%fused_computation.61 | loop fusion | flops 3145728 | bytes 529920 | tf_op jit(solution)/shard_map/convert_element_type | solution.py:48
  52.3 0.9 fusion.56
  53.5 1.1 convolution_add_fusion.3
  54.6 1.1 fusion.83
  55.7 3.3 %collective-permute-start.1 = (bf16[20,64,128]{2,1,0:T(8,128)(2,1)S(1)}, bf16[20,64,128]{2,1,0:T(8,128)(2,1)S(1)}, u32[]{:S(2)}, u32[]{:S(2)}) collective-permute-start(bf16[20,64,128]{2,1,0:T(8,128)(2,1)S(1)} %get-tuple-element.39), channel_id=1, source_target_pairs={{0,4},{4,8},{8,12},{1,5},{5,9},{9,13},{2,6},{6,10},{10,14},{3,7},{... | collective-permute-start | bytes 983048 | tf_op jit(solution)/shard_map/ppermute | solution.py:32
  59.1 1.7 %fusion.17 = f32[256,20,64]{0,2,1:T(8,128)S(1)} fusion(bf16[256,20,64]{0,2,1:T(8,128)(2,1)S(1)} %bitcast.86, f32[20,256]{1,0:T(8,128)S(1)} %copy-done.13, f32[256,256]{1,0:T(8,128)S(1)} %copy-done.4, f32[20,256]{1,0:T(8,128)S(1)} %bitcast.94, pred[256,256]{1,0:T(8,128)(4,1)S(1)} %copy-done.11), kind=kOutput, calls=%fused_computation.28 | convolution fusion | flops 175636480 | bytes 2334720 | tf_op jit(solution)/shard_map/hij,jhp->ihp/dot_general | solution.py:61
  60.9 3.9 %collective-permute-done.1 = bf16[20,64,128]{2,1,0:T(8,128)(2,1)S(1)} collective-permute-done((bf16[20,64,128]{2,1,0:T(8,128)(2,1)S(1)}, bf16[20,64,128]{2,1,0:T(8,128)(2,1)S(1)}, u32[]{:S(2)}, u32[]{:S(2)}) %collective-permute-start.1) | collective-permute-done | bytes 327712 | tf_op jit(solution)/shard_map/ppermute | solution.py:32
  65.0 10.0 %collective-permute-start.2 = (bf16[20,64,128]{2,1,0:T(8,128)(2,1)S(1)}, bf16[20,64,128]{2,1,0:T(8,128)(2,1)S(1)}, u32[]{:S(2)}, u32[]{:S(2)}) collective-permute-start(bf16[20,64,128]{2,1,0:T(8,128)(2,1)S(1)} %fusion.28), channel_id=1, source_target_pairs={{0,8},{4,12},{1,9},{5,13},{2,10},{6,14},{3,11},{7,15},{16,24},{20,... | collective-permute-start | bytes 983048 | tf_op jit(solution)/shard_map/ppermute | solution.py:32
  75.0 2.9 %fusion.18 = f32[256,20,64]{0,2,1:T(8,128)} fusion(bf16[256,20,64]{0,2,1:T(8,128)(2,1)S(1)} %bitcast.84, f32[20,256]{1,0:T(8,128)S(1)} %copy-done.12, f32[256,256]{1,0:T(8,128)S(1)} %fusion.60, f32[20,256]{1,0:T(8,128)S(1)} %bitcast.91, pred[256,256]{1,0:T(8,128)(4,1)S(1)} %copy-done.11), kind=kOutput, calls=%fused_computation.29 | convolution fusion | flops 175636480 | bytes 2334720 | tf_op jit(solution)/shard_map/hij,jhp->ihp/dot_general | solution.py:61
  77.9 1.6 %collective-permute-done.2 = bf16[20,64,128]{2,1,0:T(8,128)(2,1)S(1)} collective-permute-done((bf16[20,64,128]{2,1,0:T(8,128)(2,1)S(1)}, bf16[20,64,128]{2,1,0:T(8,128)(2,1)S(1)}, u32[]{:S(2)}, u32[]{:S(2)}) %collective-permute-start.2) | collective-permute-done | bytes 327712 | tf_op jit(solution)/shard_map/ppermute | solution.py:32
  79.9 1.5 %fusion.22 = f32[256,20,64]{0,2,1:T(8,128)} fusion(f32[256,20,64]{0,2,1:T(8,128)S(1)} %fusion.17, f32[256,20,64]{0,2,1:T(8,128)S(1)} %fusion.48, f32[256,20]{0,1:T(8,128)S(1)} %copy-done.10, bf16[512,256]{1,0:T(8,128)(2,1)S(1)} %divide_convert_fusion.1, f32[20,64,128]{2,1,0:T(8,128)S(1)} %convolution_add_fusion.3, ...), kind=kOutput, calls=%fused_computation.35 | convolution fusion | flops 86507520 | bytes 5334016 | tf_op jit(solution)/shard_map/is,hps->ihp/dot_general | solution.py:92
  81.4 1.7 %copy.76 = f32[256,1280]{1,0:T(8,128)S(1)} copy(f32[256,1280]{0,1:T(8,128)} %bitcast.82) | data formatting | bytes 2621440 | tf_op jit(solution)/shard_map/concatenate | solution.py:153
  83.5 0.9 copy-done.2
  84.4 2.2 %fusion.21 = f32[256,20,64]{0,2,1:T(8,128)} fusion(f32[256,20,64]{0,2,1:T(8,128)S(1)} %copy-done.2, f32[256,20,64]{0,2,1:T(8,128)S(1)} %fusion.37, f32[256,20]{0,1:T(8,128)} %get-tuple-element.29, bf16[20,64,128]{2,1,0:T(8,128)(2,1)S(1)} %collective-permute-done.1, bf16[20,64,128]{2,1,0:T(8,128)(2,1)S(1)} %collective-permute-done.2, f32[20]{0:T(128)S(1)} %exp.71, ...), kind=kOutput, calls=%fused_computation.34 | convolution fusion | flops 85688320 | bytes 4674048 | tf_op jit(solution)/shard_map/is,hps->ihp/dot_general | solution.py:91
  86.6 2.8 %copy.75 = f32[256,1280]{1,0:T(8,128)} copy(f32[256,1280]{0,1:T(8,128)} %bitcast.81) | data formatting | bytes 2621440 | tf_op jit(solution)/shard_map/concatenate | solution.py:153
  89.4 4.2 %multiply_reduce_fusion = (f32[512]{0:T(512)S(1)}, f32[512,1280]{1,0:T(8,128)}) fusion(bf16[512,1280]{1,0:T(8,128)(2,1)} %param.14, bf16[512,1280]{1,0:T(8,128)(2,1)S(1)} %divide_convert_fusion, f32[1280]{0:T(1024)S(1)} %mul.353, f32[256,1280]{1,0:T(8,128)S(1)} %copy.76, f32[256,1280]{1,0:T(8,128)} %copy.75), kind=kLoop, calls=%fused_computation.12 | loop fusion | flops 7208448 | bytes 7871488 | tf_op jit(solution)/shard_map/reduce_sum | solution.py:157
  93.7 5.8 %psum.7 = f32[512]{0:T(512)S(1)} all-reduce(f32[512]{0:T(512)S(1)} %get-tuple-element.12), channel_id=1, replica_groups=mesh['groups'=2,'seq'=4,'tensor'=4] {'tensor'}, use_global_device_ids=true, to_apply=%region_5.6 | all-reduce | flops 512 | bytes 4096 | tf_op jit(solution)/shard_map/psum | solution.py:157
  99.5 2.0 %multiply_convert_fusion.4 = bf16[512,1280]{1,0:T(8,128)(2,1)S(1)} fusion(f32[512,1280]{1,0:T(8,128)} %get-tuple-element.13, f32[1280]{0:T(1024)S(1)} %copy-done.14, f32[512]{0:T(512)S(1)} %add_rsqrt_fusion), kind=kLoop, calls=%fused_computation.11 | loop fusion | flops 1966080 | bytes 3939328 | tf_op jit(solution)/shard_map/convert_element_type | solution.py:161
  101.6 0.9 gather_fusion
  105.8 3.4 %collective-permute-start.5 = (bf16[40,1280]{1,0:T(8,128)(2,1)S(1)}, bf16[40,1280]{1,0:T(8,128)(2,1)S(1)}, u32[]{:S(2)}, u32[]{:S(2)}) collective-permute-start(bf16[40,1280]{1,0:T(8,128)(2,1)S(1)} %copy.90), channel_id=1, source_target_pairs={{0,8},{4,12},{8,0},{12,4},{1,9},{5,13},{9,1},{13,5},{2,10},{6,14},... | collective-permute-start | bytes 307208 | tf_op jit(solution)/shard_map/ppermute | solution.py:24
  109.4 1.5 %collective-permute-start.6 = (bf16[40,1280]{1,0:T(8,128)(2,1)S(1)}, bf16[40,1280]{1,0:T(8,128)(2,1)S(1)}, u32[]{:S(2)}, u32[]{:S(2)}) collective-permute-start(bf16[40,1280]{1,0:T(8,128)(2,1)S(1)} %copy.91), channel_id=1, source_target_pairs={{0,12},{4,8},{8,4},{12,0},{1,13},{5,9},{9,5},{13,1},{2,14},{6,10},... | collective-permute-start | bytes 307208 | tf_op jit(solution)/shard_map/ppermute | solution.py:24
  111.0 0.7 reshape.266
  111.7 3.6 %all-to-all-start = ((f32[4,1,640]{2,1,0:T(1,128)}), f32[4,1,640]{2,1,0:T(1,128)S(1)}, u32[]{:S(2)}, u32[]{:S(2)}) async-start(f32[4,1,640]{2,1,0:T(1,128)} %reshape.266), calls=%async_computation | async-start | bytes 20480 | tf_op jit(solution)/shard_map/all_to_all | solution.py:189
  115.4 5.5 %all-to-all-done = f32[4,1,640]{2,1,0:T(1,128)S(1)} async-done(((f32[4,1,640]{2,1,0:T(1,128)}), f32[4,1,640]{2,1,0:T(1,128)S(1)}, u32[]{:S(2)}, u32[]{:S(2)}) %all-to-all-start) | async-done | bytes 10272 | tf_op jit(solution)/shard_map/all_to_all | solution.py:189
  121.4 0.7 reduce.17
  122.5 0.8 reshape.234
  123.6 0.8 div.34
  (104 shorter events, 8.0 us)
Async XLA Ops:
  0.6 47.6 %copy-start.1 = (bf16[512,1280]{1,0:T(8,128)(2,1)S(1)}, bf16[512,1280]{1,0:T(8,128)(2,1)}, u32[]{:S(2)}) copy-start(bf16[512,1280]{1,0:T(8,128)(2,1)} %param.13) | copy-start | bytes 3932164
  2.2 46.0 %collective-permute-start = (bf16[3,1536]{1,0:T(4,128)(2,1)S(1)}, bf16[3,1536]{1,0:T(4,128)(2,1)S(1)}, u32[]{:S(2)}, u32[]{:S(2)}) collective-permute-start(bf16[3,1536]{1,0:T(4,128)(2,1)S(1)} %pad_maximum_fusion.3), channel_id=1, source_target_pairs={{0,4},{4,8},{8,12},{1,5},{5,9},{9,13},{2,6},{6,10},{10,14},{3,7},{... | collective-permute-start | bytes 27656 | tf_op jit(solution)/shard_map/ppermute | solution.py:32
  8.9 9.7 %copy-start.6 = (f32[3,8,2,128]{3,1,2,0:T(8,128)}, f32[3,8,2,128]{3,1,2,0:T(8,128)S(1)}, u32[]{:S(2)}) copy-start(f32[3,8,2,128]{3,1,2,0:T(8,128)S(1)} %copy.92) | copy-start | bytes 73732
  9.8 8.8 %copy-start.8 = (f32[3,8,2,128]{3,1,2,0:T(8,128)}, f32[3,8,2,128]{3,1,2,0:T(8,128)S(1)}, u32[]{:S(2)}) copy-start(f32[3,8,2,128]{3,1,2,0:T(8,128)S(1)} %copy.93) | copy-start | bytes 73732
  10.6 37.6 %collective-permute-start.3 = (f32[20]{0:T(128)S(1)}, f32[20]{0:T(128)S(1)}, u32[]{:S(2)}, u32[]{:S(2)}) collective-permute-start(f32[20]{0:T(128)S(1)} %get-tuple-element.37), channel_id=1, source_target_pairs={{0,4},{4,8},{8,12},{1,5},{5,9},{9,13},{2,6},{6,10},{10,14},{3,7},{... | collective-permute-start | bytes 248 | tf_op jit(solution)/shard_map/ppermute | solution.py:32
  53.5 5.5 %copy-start.4 = (f32[256,256]{1,0:T(8,128)S(1)}, f32[256,256]{1,0:T(8,128)}, u32[]{:S(2)}) copy-start(f32[256,256]{1,0:T(8,128)} %fusion.56) | copy-start | bytes 786436
  53.5 5.5 %copy-start.9 = (f32[3,8,2,128]{3,1,2,0:T(8,128)S(1)}, f32[3,8,2,128]{3,1,2,0:T(8,128)}, u32[]{:S(2)}) copy-start(f32[3,8,2,128]{3,1,2,0:T(8,128)} %copy-done.8) | copy-start | bytes 73732
  53.5 5.5 %copy-start.11 = (pred[256,256]{1,0:T(8,128)(4,1)S(1)}, pred[256,256]{1,0:T(8,128)(4,1)}, u32[]{:S(2)}) copy-start(pred[256,256]{1,0:T(8,128)(4,1)} %iota_compare_fusion) | copy-start | bytes 196612
  53.5 5.5 %copy-start.13 = (f32[20,256]{1,0:T(8,128)S(1)}, f32[20,256]{1,0:T(8,128)}, u32[]{:S(2)}) copy-start(f32[20,256]{1,0:T(8,128)} %get-tuple-element.25) | copy-start | bytes 61444
  55.7 9.1 %collective-permute-start.1 = (bf16[20,64,128]{2,1,0:T(8,128)(2,1)S(1)}, bf16[20,64,128]{2,1,0:T(8,128)(2,1)S(1)}, u32[]{:S(2)}, u32[]{:S(2)}) collective-permute-start(bf16[20,64,128]{2,1,0:T(8,128)(2,1)S(1)} %get-tuple-element.39), channel_id=1, source_target_pairs={{0,4},{4,8},{8,12},{1,5},{5,9},{9,13},{2,6},{6,10},{10,14},{3,7},{... | collective-permute-start | bytes 983048 | tf_op jit(solution)/shard_map/ppermute | solution.py:32
  59.0 5.8 %copy-start.16 = (f32[20]{0:T(128)S(1)}, f32[20]{0:T(128)}, u32[]{:S(2)}) copy-start(f32[20]{0:T(128)} %get-tuple-element.36) | copy-start | bytes 244
  59.0 15.9 %copy-start.7 = (f32[3,8,2,128]{3,1,2,0:T(8,128)S(1)}, f32[3,8,2,128]{3,1,2,0:T(8,128)}, u32[]{:S(2)}) copy-start(f32[3,8,2,128]{3,1,2,0:T(8,128)} %copy-done.6) | copy-start | bytes 73732
  59.0 15.9 %copy-start.12 = (f32[20,256]{1,0:T(8,128)S(1)}, f32[20,256]{1,0:T(8,128)}, u32[]{:S(2)}) copy-start(f32[20,256]{1,0:T(8,128)} %get-tuple-element.22) | copy-start | bytes 61444
  65.0 14.5 %collective-permute-start.2 = (bf16[20,64,128]{2,1,0:T(8,128)(2,1)S(1)}, bf16[20,64,128]{2,1,0:T(8,128)(2,1)S(1)}, u32[]{:S(2)}, u32[]{:S(2)}) collective-permute-start(bf16[20,64,128]{2,1,0:T(8,128)(2,1)S(1)} %fusion.28), channel_id=1, source_target_pairs={{0,8},{4,12},{1,9},{5,13},{2,10},{6,14},{3,11},{7,15},{16,24},{20,... | collective-permute-start | bytes 983048 | tf_op jit(solution)/shard_map/ppermute | solution.py:32
  75.0 4.5 %copy-start.15 = (f32[20]{0:T(128)S(1)}, f32[20]{0:T(128)}, u32[]{:S(2)}) copy-start(f32[20]{0:T(128)} %get-tuple-element.34) | copy-start | bytes 244
  77.9 2.0 %copy-start.10 = (f32[256,20]{0,1:T(8,128)S(1)}, f32[256,20]{0,1:T(8,128)}, u32[]{:S(2)}) copy-start(f32[256,20]{0,1:T(8,128)} %get-tuple-element.28) | copy-start | bytes 61444
  83.1 1.3 %copy-start.2 = (f32[256,20,64]{0,2,1:T(8,128)S(1)}, f32[256,20,64]{0,2,1:T(8,128)}, u32[]{:S(2)}) copy-start(f32[256,20,64]{0,2,1:T(8,128)} %fusion.18) | copy-start | bytes 3932164
  89.4 10.1 %copy-start.14 = (f32[1280]{0:T(1024)S(1)}, f32[1280]{0:T(1024)}, u32[]{:S(2)}) copy-start(f32[1280]{0:T(1024)} %param.21) | copy-start | bytes 15364
  101.5 2.1 %copy-start = (bf16[512,1280]{1,0:T(8,128)(2,1)}, bf16[512,1280]{1,0:T(8,128)(2,1)S(1)}, u32[]{:S(2)}) copy-start(bf16[512,1280]{1,0:T(8,128)(2,1)S(1)} %multiply_convert_fusion.4) | copy-start | bytes 3932164
  101.5 1.6 %copy-start.3 = (bf16[160,8,160]{2,1,0:T(8,128)(2,1)S(1)}, bf16[160,8,160]{2,1,0:T(8,128)(2,1)}, u32[]{:S(2)}) copy-start(bf16[160,8,160]{2,1,0:T(8,128)(2,1)} %reshape.221) | copy-start | bytes 1228804
  101.6 1.6 %copy-start.5 = (pred[160,128]{1,0:T(8,128)(4,1)S(1)}, pred[160,128]{1,0:T(8,128)(4,1)}, u32[]{:S(2)}) copy-start(pred[160,128]{1,0:T(8,128)(4,1)} %compare_and_fusion) | copy-start | bytes 61444
  101.6 1.5 %copy-start.17 = (pred[128]{0:T(512)(128)(4,1)S(1)}, pred[128]{0:T(512)(128)(4,1)}, u32[]{:S(2)}) copy-start(pred[128]{0:T(512)(128)(4,1)} %get-tuple-element.10) | copy-start | bytes 388
  105.5 16.9 %collective-permute-start.4 = (bf16[40,1280]{1,0:T(8,128)(2,1)S(1)}, bf16[40,1280]{1,0:T(8,128)(2,1)S(1)}, u32[]{:S(2)}, u32[]{:S(2)}) collective-permute-start(bf16[40,1280]{1,0:T(8,128)(2,1)S(1)} %copy.89), channel_id=1, source_target_pairs={{0,4},{4,0},{8,12},{12,8},{1,5},{5,1},{9,13},{13,9},{2,6},{6,2},{1... | collective-permute-start | bytes 307208 | tf_op jit(solution)/shard_map/ppermute | solution.py:24
  105.8 16.7 %collective-permute-start.5 = (bf16[40,1280]{1,0:T(8,128)(2,1)S(1)}, bf16[40,1280]{1,0:T(8,128)(2,1)S(1)}, u32[]{:S(2)}, u32[]{:S(2)}) collective-permute-start(bf16[40,1280]{1,0:T(8,128)(2,1)S(1)} %copy.90), channel_id=1, source_target_pairs={{0,8},{4,12},{8,0},{12,4},{1,9},{5,13},{9,1},{13,5},{2,10},{6,14},... | collective-permute-start | bytes 307208 | tf_op jit(solution)/shard_map/ppermute | solution.py:24
  109.4 13.1 %collective-permute-start.6 = (bf16[40,1280]{1,0:T(8,128)(2,1)S(1)}, bf16[40,1280]{1,0:T(8,128)(2,1)S(1)}, u32[]{:S(2)}, u32[]{:S(2)}) collective-permute-start(bf16[40,1280]{1,0:T(8,128)(2,1)S(1)} %copy.91), channel_id=1, source_target_pairs={{0,12},{4,8},{8,4},{12,0},{1,13},{5,9},{9,5},{13,1},{2,14},{6,10},... | collective-permute-start | bytes 307208 | tf_op jit(solution)/shard_map/ppermute | solution.py:24
  111.7 9.2 %all-to-all-start = ((f32[4,1,640]{2,1,0:T(1,128)}), f32[4,1,640]{2,1,0:T(1,128)S(1)}, u32[]{:S(2)}, u32[]{:S(2)}) async-start(f32[4,1,640]{2,1,0:T(1,128)} %reshape.266), calls=%async_computation | async-start | bytes 20480 | tf_op jit(solution)/shard_map/all_to_all | solution.py:189
